TPU v7x, 32 devices: a whole 2x2x4 slice. The times are simulated.
32 devices in a mesh: parts: 2 (over y), seq: 4 (over z), section: 2 (over x), tp: 2 (over core).
Axes of the slice: x: 2, y: 2, z: 4, core: 2. Of those that a mesh axis runs over, the one named last changes fastest.
Arguments:
- queries: bfloat16 [2, 2048, 4096], P('section', ('parts', 'seq'), 'tp'), parts along dimension 1, may hold values from -82 to 82
- keys_values: bfloat16 [2, 2, 2048, 512], P('section', None, ('parts', 'seq'), 'tp'), parts along dimension 2, may hold values from -4 to 4
- lengths: int32 [2], P('parts'), parts along dimension 0, may hold values from 769 to 1024, as said below
Outputs:
- attended: bfloat16 [2, 2048, 4096], P('section', ('parts', 'seq'), 'tp'), parts along dimension 1
- window_cache: bfloat16 [2, 2, 4096, 512], P('section', None, ('parts', 'seq'), 'tp'), parts along dimension 2
There are 2 independent parts, one for each index of `parts`. A program takes and returns all parts, laid end to end along the dimension named above; each array names one. Nothing has to cross between parts.
Inputs may be any that keep to these rules, and one draw needn't show every extreme that they name: `lengths`: the first request's length lies in min(2048, 1024 - 256) + 1 to min(2048, 1024 - 256) + 256; the second request's length is 1024.
All inputs are finite; a program needn't handle non-finite values.
Results may differ from a plain program's by a relative error of at most 0.0077.
Values may be sent and summed in bfloat16 or wider, within the bound.
No kernel may reach another device: no remote copies, remote signals or barrier semaphores. Data moves between devices by JAX's collectives and lax.ppermute only.
A program may use at most 64 MiB of HBM per device.

v0:
```python
import math
import jax
import jax.numpy as jnp
from jax import lax
from jax.sharding import PartitionSpec as P

HD = 128
WINDOW = 2048
rope_base = 1000000.0
neg_floor = -1e30


def passed_along(x, axis, by):
    devices = lax.axis_size(axis)
    pairs = [(i, i + by) for i in range(devices) if 0 <= i + by < devices]
    return lax.ppermute(x, axis, pairs)


def rotate(field, positions):
    half_dim = field.shape[-1] // 2
    frequency = jnp.exp(
        jnp.arange(half_dim, dtype=jnp.float32) * (-2.0 * math.log(rope_base) / field.shape[-1])
    )
    angles = positions.astype(jnp.float32)[:, None] * frequency[None, :]
    cosine = jnp.cos(angles)[:, None, :]
    sine_part = jnp.sin(angles)[:, None, :]
    lower_half = field[..., :half_dim]
    upper_half = field[..., half_dim:]
    return jnp.concatenate(
        [
            lower_half * cosine - upper_half * sine_part,
            upper_half * cosine + lower_half * sine_part,
        ],
        axis=-1,
    )


def local(queries, keys_values, lengths):
    seq_len = lengths[0]
    shard_rows = queries.shape[1]
    width = keys_values.shape[-1]
    kv_heads_dev = width // HD
    heads_dev = queries.shape[-1] // HD
    group_size = heads_dev // kv_heads_dev
    seq_index = lax.axis_index("seq")
    seq_count = lax.axis_size("seq")
    first_pos = seq_index * shard_rows
    positions = first_pos + jnp.arange(shard_rows, dtype=jnp.int32)
    scale = 1.0 / math.sqrt(HD)
    rotated_q = rotate(queries[0].reshape(shard_rows, heads_dev, HD).astype(jnp.float32), positions)
    rotated_q = rotated_q.astype(jnp.bfloat16).reshape(shard_rows, kv_heads_dev, group_size, HD)
    rotated_k = rotate(
        keys_values[0, 0].reshape(shard_rows, kv_heads_dev, HD).astype(jnp.float32), positions
    )
    own_block = jnp.stack(
        [rotated_k.astype(jnp.bfloat16).reshape(shard_rows, width), keys_values[0, 1]]
    )

    def attend(state_now, kv_piece, start_pos):
        row_top, totals, numer_acc = state_now
        piece_rows = kv_piece.shape[1]
        key_pos = start_pos + jnp.arange(piece_rows, dtype=jnp.int32)
        key_rows = kv_piece[0].reshape(piece_rows, kv_heads_dev, HD)
        value_rows = kv_piece[1].reshape(piece_rows, kv_heads_dev, HD)
        scores = (
            jnp.einsum("qkgd,skd->kgqs", rotated_q, key_rows, preferred_element_type=jnp.float32)
            * scale
        )
        allowed = (key_pos[None, :] <= positions[:, None]) & (
            key_pos[None, :] > positions[:, None] - WINDOW
        )
        allowed = allowed & (key_pos[None, :] >= 0) & (key_pos[None, :] < seq_len)
        top_new = jnp.maximum(row_top, jnp.max(jnp.where(allowed, scores, neg_floor), axis=-1))
        weights = jnp.where(allowed, jnp.exp(scores - top_new[..., None]), 0.0)
        rescale = jnp.exp(row_top - top_new)
        totals = totals * rescale + jnp.sum(weights, axis=-1)
        update = jnp.einsum(
            "kgqs,skd->qkgd",
            weights.astype(jnp.bfloat16),
            value_rows,
            preferred_element_type=jnp.float32,
        )
        numer_acc = numer_acc * jnp.moveaxis(rescale, 2, 0)[..., None] + update
        return (top_new, totals, numer_acc)

    start_state = (
        jnp.full((kv_heads_dev, group_size, shard_rows), neg_floor, jnp.float32),
        jnp.zeros((kv_heads_dev, group_size, shard_rows), jnp.float32),
        jnp.zeros((shard_rows, kv_heads_dev, group_size, HD), jnp.float32),
    )
    reach_count = min(WINDOW // shard_rows, seq_count - 1)
    tail_start = first_pos - reach_count * shard_rows
    older_blocks = []
    moving = own_block
    for hop in range(reach_count):
        moving = passed_along(moving, "seq", 1)
        older_blocks.insert(0, moving)
    tail_rows = jnp.concatenate(older_blocks + [own_block], axis=1)
    piece_count = tail_rows.shape[1] // shard_rows
    limit_rows = max(1024, shard_rows)
    multiple = max(
        (
            divisor
            for divisor in range(1, piece_count + 1)
            if piece_count % divisor == 0 and divisor * shard_rows <= limit_rows
        )
    )
    key_block = multiple * shard_rows

    def key_step(blk_index, state_now):
        kv_piece = lax.dynamic_slice_in_dim(tail_rows, blk_index * key_block, key_block, 1)
        return attend(state_now, kv_piece, tail_start + blk_index * key_block)

    final_state = lax.fori_loop(0, tail_rows.shape[1] // key_block, key_step, start_state)
    row_top, totals, numer_acc = final_state
    valid = positions < seq_len
    denom = jnp.where(valid[:, None, None], jnp.moveaxis(totals, 2, 0), 1.0)
    result = jnp.where(valid[:, None, None, None], numer_acc / denom[..., None], 0.0)
    attended = result.astype(jnp.bfloat16).reshape(1, shard_rows, heads_dev * HD)
    slot_rows = WINDOW // seq_count
    zero_pad = jnp.zeros((2, WINDOW, width), jnp.bfloat16)
    padded_own = jnp.concatenate([zero_pad, own_block, zero_pad], axis=1)
    begin_row = jnp.clip(seq_len - first_pos, 0, WINDOW + shard_rows)
    outbox = lax.dynamic_slice_in_dim(padded_own, begin_row, WINDOW, 1)
    received = lax.all_to_all(outbox, "seq", split_axis=1, concat_axis=1, tiled=True)
    window_cache = (
        received.reshape(2, seq_count, slot_rows, width)
        .astype(jnp.float32)
        .sum(axis=1)
        .astype(jnp.bfloat16)
    )
    return (attended, window_cache[None])


def solution(mesh):
    return jax.shard_map(
        local,
        mesh=mesh,
        in_specs=(
            P("section", ("parts", "seq"), "tp"),
            P("section", None, ("parts", "seq"), "tp"),
            P("parts"),
        ),
        out_specs=(
            P("section", ("parts", "seq"), "tp"),
            P("section", None, ("parts", "seq"), "tp"),
        ),
        check_vma=False,
    )
```

profile of v0, /device:TPU:20, one launch (start us, length us, event | category | flops | bytes accessed | tf_op | source)
XLA Modules:
  0.0 137.0 jit_solution(13391435506342000637)
XLA Ops:
  0.6 1.0 slice_convert_fusion
  2.3 0.7 pad_maximum_fusion
  3.0 3.5 %collective-permute-start = (bf16[2,256,256]{1,2,0:T(8,128)(2,1)}, bf16[2,256,256]{1,2,0:T(8,128)(2,1)}, u32[]{:S(2)}, u32[]{:S(2)}) collective-permute-start(bf16[2,256,256]{1,2,0:T(8,128)(2,1)} %pad_maximum_fusion), channel_id=1, source_target_pairs={{0,4},{4,8},{8,12},{1,5},{5,9},{9,13},{2,6},{6,10},{10,14},{3,7},{... | collective-permute-start | bytes 786440 | tf_op jit(solution)/shard_map/ppermute | solution.py:16
  6.5 1.1 copy.53
  8.3 1.1 broadcast_in_dim.84
  9.4 30.1 %fusion.9 = bf16[2,2048,256]{2,0,1:T(2,128)(2,1)} fusion(s32[]{:T(128)S(6)} %min.4, bf16[2,2048,256]{2,0,1:T(2,128)(2,1)S(1)} %broadcast_in_dim.84, bf16[2,256,256]{2,0,1:T(2,128)(2,1)S(1)} %copy.53), kind=kLoop, calls=%fused_computation.13 | loop fusion | flops 2097152 | bytes 4456452 | tf_op jit(solution)/shard_map/concatenate | solution.py:122
  39.5 4.7 %all-to-all-start = ((bf16[2,2048,256]{2,0,1:T(2,128)(2,1)}), bf16[2,2048,256]{2,0,1:T(2,128)(2,1)S(1)}, u32[]{:S(2)}, u32[]{:S(2)}) async-start(bf16[2,2048,256]{2,0,1:T(2,128)(2,1)} %fusion.9), calls=%async_computation | async-start | bytes 4194304 | tf_op jit(solution)/shard_map/all_to_all | solution.py:125
  44.2 0.8 copy.50
  45.0 0.7 copy.48
  46.0 0.4 copy.65
  46.4 0.7 fusion.28
  47.1 3.4 %collective-permute-start.1 = (bf16[2,256,256]{1,2,0:T(8,128)(2,1)}, bf16[2,256,256]{1,2,0:T(8,128)(2,1)S(1)}, u32[]{:S(2)}, u32[]{:S(2)}) collective-permute-start(bf16[2,256,256]{1,2,0:T(8,128)(2,1)} %collective-permute-done), channel_id=1, source_target_pairs={{0,4},{4,8},{8,12},{1,5},{5,9},{9,13},{2,6},{6,10},{10,14},{3,7},{... | collective-permute-start | bytes 786440 | tf_op jit(solution)/shard_map/ppermute | solution.py:16
  50.5 1.4 subtract_convert_fusion
  51.9 43.8 %collective-permute-done.1 = bf16[2,256,256]{1,2,0:T(8,128)(2,1)S(1)} collective-permute-done((bf16[2,256,256]{1,2,0:T(8,128)(2,1)}, bf16[2,256,256]{1,2,0:T(8,128)(2,1)S(1)}, u32[]{:S(2)}, u32[]{:S(2)}) %collective-permute-start.1) | collective-permute-done | bytes 262176 | tf_op jit(solution)/shard_map/ppermute | solution.py:16
  95.7 2.1 %collective-permute-start.2 = (bf16[2,256,256]{1,2,0:T(8,128)(2,1)S(1)}, bf16[2,256,256]{1,2,0:T(8,128)(2,1)S(1)}, u32[]{:S(2)}, u32[]{:S(2)}) collective-permute-start(bf16[2,256,256]{1,2,0:T(8,128)(2,1)S(1)} %collective-permute-done.1), channel_id=1, source_target_pairs={{0,4},{4,8},{8,12},{1,5},{5,9},{9,13},{2,6},{6,10},{10,14},{3,7},{... | collective-permute-start | bytes 786440 | tf_op jit(solution)/shard_map/ppermute | solution.py:16
  97.8 0.9 and_and_fusion
  98.7 5.7 %collective-permute-done.2 = bf16[2,256,256]{1,2,0:T(8,128)(2,1)S(1)} collective-permute-done((bf16[2,256,256]{1,2,0:T(8,128)(2,1)S(1)}, bf16[2,256,256]{1,2,0:T(8,128)(2,1)S(1)}, u32[]{:S(2)}, u32[]{:S(2)}) %collective-permute-start.2) | collective-permute-done | bytes 262176 | tf_op jit(solution)/shard_map/ppermute | solution.py:16
  104.4 1.1 maximum_maximum_fusion
  105.6 7.7 %fusion = (f32[2,8,256]{2,1,0:T(8,128)S(1)}, f32[2,1024,256,8]{2,1,3,0:T(8,128)}) fusion(pred[256,1024]{0,1:T(8,128)(4,1)S(1)} %and_and_fusion, bf16[1024,2,128,1]{0,2,3,1:T(8,128)(2,1)S(1)} %bitcast.64, bf16[256,2,8,64]{3,0,2,1:T(8,128)(2,1)S(1)} %bitcast.63, bf16[256,2,8,64]{3,0,2,1:T(8,128)(2,1)S(1)} %bitcast.62), kind=kOutput, calls=%fused_computation.2 | convolution fusion | flops 1088417792 | bytes 18628608 | tf_op jit(solution)/shard_map/while/body/eval_jaxpr/qkgd,skd->kgqs/dot_general | solution.py:66
  113.3 9.1 %fusion.3 = f32[2,8,256]{2,1,0:T(8,128)S(1)} fusion(f32[2,1024,256,8]{2,1,3,0:T(8,128)} %get-tuple-element.57, f32[2,8,256]{2,1,0:T(8,128)S(1)} %get-tuple-element.53, pred[256,1024]{0,1:T(8,128)(4,1)S(1)} %and_and_fusion), kind=kLoop, calls=%fused_computation.5 | loop fusion | flops 16773120 | bytes 17072128 | tf_op jit(solution)/shard_map/while/body/eval_jaxpr/reduce_sum | solution.py:76
  122.4 9.4 %fusion.12 = bf16[256,2,8,128]{0,3,2,1:T(8,128)(2,1)S(1)} fusion(bf16[1024,2,128,1]{0,2,3,1:T(8,128)(2,1)S(1)} %bitcast.72, f32[2,1024,256,8]{2,1,3,0:T(8,128)} %get-tuple-element.57, f32[2,8,256]{2,1,0:T(8,128)S(1)} %get-tuple-element.53, pred[256,1024]{0,1:T(8,128)(4,1)S(1)} %and_and_fusion, f32[256,2,8]{0,2,1:T(8,128)S(1)} %fusion.19, ...), kind=kOutput, calls=%fused_computation.17 | convolution fusion | flops 1092616192 | bytes 18661632 | tf_op jit(solution)/shard_map/while/body/eval_jaxpr/kgqs,skd->qkgd/dot_general | solution.py:77
  131.8 1.4 %copy.54 = bf16[1,256,2048]{2,1,0:T(8,128)(2,1)} copy(bf16[1,256,2048]{1,2,0:T(8,128)(2,1)S(1)} %bitcast.70) | data formatting | bytes 2097152
  133.2 2.9 %reduce_sum.26 = bf16[2,512,256]{2,0,1:T(2,128)(2,1)S(1)} reduce(bf16[2,4,512,256]{3,0,2,1:T(2,128)(2,1)S(1)} %bitcast.61, bf16[]{:T(256)} %constant.50.clone.1), dimensions={1}, to_apply=%region_2.0 | reduce | flops 786432 | bytes 2621442 | tf_op jit(solution)/shard_map/reduce_sum | solution.py:129
  136.2 0.9 copy.55
  (23 shorter events, 1.0 us)
Async XLA Ops:
  3.0 44.1 %collective-permute-start = (bf16[2,256,256]{1,2,0:T(8,128)(2,1)}, bf16[2,256,256]{1,2,0:T(8,128)(2,1)}, u32[]{:S(2)}, u32[]{:S(2)}) collective-permute-start(bf16[2,256,256]{1,2,0:T(8,128)(2,1)} %pad_maximum_fusion), channel_id=1, source_target_pairs={{0,4},{4,8},{8,12},{1,5},{5,9},{9,13},{2,6},{6,10},{10,14},{3,7},{... | collective-permute-start | bytes 786440 | tf_op jit(solution)/shard_map/ppermute | solution.py:16
  39.5 6.2 %copy-start = (bf16[1,256,2048]{2,1,0:T(8,128)(2,1)S(1)}, bf16[1,256,2048]{2,1,0:T(8,128)(2,1)}, u32[]{:S(2)}) copy-start(bf16[1,256,2048]{2,1,0:T(8,128)(2,1)} %param.3) | copy-start | bytes 3145732
  39.5 93.7 %all-to-all-start = ((bf16[2,2048,256]{2,0,1:T(2,128)(2,1)}), bf16[2,2048,256]{2,0,1:T(2,128)(2,1)S(1)}, u32[]{:S(2)}, u32[]{:S(2)}) async-start(bf16[2,2048,256]{2,0,1:T(2,128)(2,1)} %fusion.9), calls=%async_computation | async-start | bytes 4194304 | tf_op jit(solution)/shard_map/all_to_all | solution.py:125
  46.4 4.1 %copy-start.1 = (f32[256,64]{1,0:T(8,128)S(1)}, f32[256,64]{1,0:T(8,128)}, u32[]{:S(2)}) copy-start(f32[256,64]{1,0:T(8,128)} %copy.50) | copy-start | bytes 196612
  46.4 4.1 %copy-start.2 = (f32[256,64]{1,0:T(8,128)S(1)}, f32[256,64]{1,0:T(8,128)}, u32[]{:S(2)}) copy-start(f32[256,64]{1,0:T(8,128)} %copy.48) | copy-start | bytes 196612
  47.1 48.6 %collective-permute-start.1 = (bf16[2,256,256]{1,2,0:T(8,128)(2,1)}, bf16[2,256,256]{1,2,0:T(8,128)(2,1)S(1)}, u32[]{:S(2)}, u32[]{:S(2)}) collective-permute-start(bf16[2,256,256]{1,2,0:T(8,128)(2,1)} %collective-permute-done), channel_id=1, source_target_pairs={{0,4},{4,8},{8,12},{1,5},{5,9},{9,13},{2,6},{6,10},{10,14},{3,7},{... | collective-permute-start | bytes 786440 | tf_op jit(solution)/shard_map/ppermute | solution.py:16
  95.7 8.7 %collective-permute-start.2 = (bf16[2,256,256]{1,2,0:T(8,128)(2,1)S(1)}, bf16[2,256,256]{1,2,0:T(8,128)(2,1)S(1)}, u32[]{:S(2)}, u32[]{:S(2)}) collective-permute-start(bf16[2,256,256]{1,2,0:T(8,128)(2,1)S(1)} %collective-permute-done.1), channel_id=1, source_target_pairs={{0,4},{4,8},{8,12},{1,5},{5,9},{9,13},{2,6},{6,10},{10,14},{3,7},{... | collective-permute-start | bytes 786440 | tf_op jit(solution)/shard_map/ppermute | solution.py:16
where the time goes:
time: 137 us
  waiting for transfers between devices  49.5 us (36%)
  other arithmetic  47.8 us (35%)
  matrix products  17.1 us (12%)
  starting transfers between devices  13.7 us (10%)
  local copies, waits for them, and re-layouts  7.42 us (5%)
  between operations  1.53 us (1%)
    ppermute x3, waiting for transfers between devices, passed_along(): return lax.ppermute(x, axis, pairs)  49.5 us
    concatenate x1, other arithmetic, local(): padded_own = jnp.concatenate([zero_pad, own_block, zero_pad], axis=1)  30.1 us
    dot_general x1, matrix products, attend(): jnp.einsum('kgqs,skd->qkgd', weights.astype(jnp.bfloat16), value_rows, pr...  9.41 us
    reduce_sum x1, other arithmetic, attend(): totals = totals * rescale + jnp.sum(weights, axis=-1)  9.12 us
    ppermute x3, starting transfers between devices, passed_along(): return lax.ppermute(x, axis, pairs)  8.94 us
    dot_general x1, matrix products, attend(): jnp.einsum('qkgd,skd->kgqs', rotated_q, key_rows, preferred_element_type=...  7.66 us
    all_to_all x1, starting transfers between devices, local(): lax.all_to_all(outbox, 'seq', split_axis=1, concat_axis=1, tiled=True)  4.73 us
    reduce_sum x1, other arithmetic, local(): window_cache = received.reshape(2, seq_count, slot_rows, width).astype(jn...  2.93 us
  transfers between devices with their start and end apart: 4, of which 2 were waited for; matrix products, arithmetic and copies ran while one was open for 48% of the time, Pallas kernels for 0%

commit v1 on v0

--- a/solution.py
+++ b/solution.py
@@ -122,7 +122,9 @@
     padded_own = jnp.concatenate([zero_pad, own_block, zero_pad], axis=1)
     begin_row = jnp.clip(seq_len - first_pos, 0, WINDOW + shard_rows)
     outbox = lax.dynamic_slice_in_dim(padded_own, begin_row, WINDOW, 1)
-    received = lax.all_to_all(outbox, "seq", split_axis=1, concat_axis=1, tiled=True)
+    pieces = jnp.split(outbox, lax.axis_size("seq"), axis=1)
+    incoming = lax.all_to_all(jnp.stack(pieces), "seq", 0, 0)
+    received = jnp.concatenate(incoming, axis=1)
     window_cache = (
         received.reshape(2, seq_count, slot_rows, width)
         .astype(jnp.float32)

time: 137 us -> 111 us (0.81)
  other arithmetic: 47.8 us -> 22.8 us
    concatenate x1, other arithmetic: 30.1 us -> 5.08 us  [local(): padded_own = jnp.concatenate([zero_pad, own_block, zero_pad], axis=1)]
    reduce_sum x1, other arithmetic: 2.93 us -> 1.24 us  [local(): window_cache = received.reshape(2, seq_count, slot_rows, width).astype(jn...]
    another operation x2 -> x3, other arithmetic: 1.39 us -> 3.02 us  [the longest x1 1.59 us: local(): incoming = lax.all_to_all(jnp.stack(pieces), 'seq', 0, 0)]
    unnamed x10 -> x11, local copies, waits for them, and re-layouts: 2.79 us -> 1.93 us
  transfers between devices with their start and end apart: 4 -> 4, of which waited for: 2 -> 2; matrix products, arithmetic and copies ran while one was open for 48% -> 39% of each run, Pallas kernels for 0% -> 0%
where the time goes in v1:
time: 111 us
  waiting for transfers between devices  49.5 us (45%)
  other arithmetic  22.8 us (21%)
  matrix products  17.1 us (15%)
  starting transfers between devices  13.7 us (12%)
  local copies, waits for them, and re-layouts  6.47 us (6%)
  between operations  1.54 us (1%)
    ppermute x3, waiting for transfers between devices, passed_along(): return lax.ppermute(x, axis, pairs)  49.5 us
    dot_general x1, matrix products, attend(): jnp.einsum('kgqs,skd->qkgd', weights.astype(jnp.bfloat16), value_rows, pr...  9.41 us
    reduce_sum x1, other arithmetic, attend(): totals = totals * rescale + jnp.sum(weights, axis=-1)  9.17 us
    ppermute x3, starting transfers between devices, passed_along(): return lax.ppermute(x, axis, pairs)  8.94 us
    dot_general x1, matrix products, attend(): jnp.einsum('qkgd,skd->kgqs', rotated_q, key_rows, preferred_element_type=...  7.65 us
    concatenate x1, other arithmetic, local(): padded_own = jnp.concatenate([zero_pad, own_block, zero_pad], axis=1)  5.08 us
    all_to_all x1, starting transfers between devices, local(): incoming = lax.all_to_all(jnp.stack(pieces), 'seq', 0, 0)  4.73 us
  transfers between devices with their start and end apart: 4, of which 2 were waited for; matrix products, arithmetic and copies ran while one was open for 39% of the time, Pallas kernels for 0%

profile of v1, /device:TPU:20, one launch (start us, length us, event | category | flops | bytes accessed | tf_op | source)
XLA Modules:
  0.0 111.1 jit_solution(1542230494412357323)
XLA Ops:
  0.6 1.0 slice_convert_fusion
  2.3 0.7 pad_maximum_fusion.1
  3.0 3.5 %collective-permute-start = (bf16[2,256,256]{1,2,0:T(8,128)(2,1)}, bf16[2,256,256]{1,2,0:T(8,128)(2,1)}, u32[]{:S(2)}, u32[]{:S(2)}) collective-permute-start(bf16[2,256,256]{1,2,0:T(8,128)(2,1)} %pad_maximum_fusion.1), channel_id=1, source_target_pairs={{0,4},{4,8},{8,12},{1,5},{5,9},{9,13},{2,6},{6,10},{10,14},{3,7},{... | collective-permute-start | bytes 786440 | tf_op jit(solution)/shard_map/ppermute | solution.py:16
  6.5 1.1 copy.41
  8.4 5.1 %fusion.9 = bf16[2,2048,256]{2,1,0:T(8,128)(2,1)S(1)} fusion(s32[]{:T(128)S(6)} %min.4, bf16[2,2048,256]{2,1,0:T(8,128)(2,1)S(1)} %broadcast_in_dim.84, bf16[2,256,256]{2,1,0:T(8,128)(2,1)S(1)} %copy.41), kind=kLoop, calls=%fused_computation.13 | loop fusion | flops 6291456 | bytes 4456452 | tf_op jit(solution)/shard_map/concatenate | solution.py:122
  13.6 1.6 %pad_maximum_fusion = bf16[4,2,512,256]{3,2,1,0:T(8,128)(2,1)} fusion(bf16[1,2,512,256]{3,2,1,0:T(8,128)(2,1)S(1)} %get-tuple-element.45, bf16[1,2,512,256]{3,2,1,0:T(8,128)(2,1)S(1)} %get-tuple-element.43, bf16[1,2,512,256]{3,2,1,0:T(8,128)(2,1)S(1)} %get-tuple-element.44, bf16[1,2,512,256]{3,2,1,0:T(8,128)(2,1)S(1)} %get-tuple-element.42), kind=kLoop, calls=%fused_computation.14 | loop fusion | flops 3145728 | bytes 4194304 | tf_op jit(solution)/shard_map/stack | solution.py:126
  15.2 4.7 %all-to-all-start = ((bf16[4,2,512,256]{3,2,1,0:T(8,128)(2,1)}), bf16[4,2,512,256]{3,2,1,0:T(8,128)(2,1)S(1)}, u32[]{:S(2)}, u32[]{:S(2)}) async-start(bf16[4,2,512,256]{3,2,1,0:T(8,128)(2,1)} %pad_maximum_fusion), calls=%async_computation | async-start | bytes 4194304 | tf_op jit(solution)/shard_map/all_to_all | solution.py:126
  20.0 0.8 copy.38
  20.7 0.7 copy.36
  21.7 0.4 copy.52
  22.2 0.7 fusion.28
  22.8 3.4 %collective-permute-start.1 = (bf16[2,256,256]{1,2,0:T(8,128)(2,1)}, bf16[2,256,256]{1,2,0:T(8,128)(2,1)S(1)}, u32[]{:S(2)}, u32[]{:S(2)}) collective-permute-start(bf16[2,256,256]{1,2,0:T(8,128)(2,1)} %collective-permute-done), channel_id=1, source_target_pairs={{0,4},{4,8},{8,12},{1,5},{5,9},{9,13},{2,6},{6,10},{10,14},{3,7},{... | collective-permute-start | bytes 786440 | tf_op jit(solution)/shard_map/ppermute | solution.py:16
  26.2 1.4 %subtract_convert_fusion = (bf16[256,16,64]{2,0,1:T(8,128)(2,1)S(1)}, bf16[256,16,64]{2,0,1:T(8,128)(2,1)S(1)}) fusion(f32[256,16,64]{2,1,0:T(8,128)S(1)} %get-tuple-element.47, f32[256,16,64]{2,1,0:T(8,128)S(1)} %get-tuple-element.46, f32[256,64]{1,0:T(8,128)S(1)} %copy-done.1, f32[256,64]{1,0:T(8,128)S(1)} %copy-done.2), kind=kLoop, calls=%fused_computation.21 | loop fusion | flops 2097152 | bytes 3276800 | tf_op jit(solution)/shard_map/convert.6
  27.6 43.8 %collective-permute-done.1 = bf16[2,256,256]{1,2,0:T(8,128)(2,1)S(1)} collective-permute-done((bf16[2,256,256]{1,2,0:T(8,128)(2,1)}, bf16[2,256,256]{1,2,0:T(8,128)(2,1)S(1)}, u32[]{:S(2)}, u32[]{:S(2)}) %collective-permute-start.1) | collective-permute-done | bytes 262176 | tf_op jit(solution)/shard_map/ppermute | solution.py:16
  71.4 2.1 %collective-permute-start.2 = (bf16[2,256,256]{1,2,0:T(8,128)(2,1)S(1)}, bf16[2,256,256]{1,2,0:T(8,128)(2,1)S(1)}, u32[]{:S(2)}, u32[]{:S(2)}) collective-permute-start(bf16[2,256,256]{1,2,0:T(8,128)(2,1)S(1)} %collective-permute-done.1), channel_id=1, source_target_pairs={{0,4},{4,8},{8,12},{1,5},{5,9},{9,13},{2,6},{6,10},{10,14},{3,7},{... | collective-permute-start | bytes 786440 | tf_op jit(solution)/shard_map/ppermute | solution.py:16
  73.5 0.9 and_and_fusion
  74.4 5.7 %collective-permute-done.2 = bf16[2,256,256]{1,2,0:T(8,128)(2,1)S(1)} collective-permute-done((bf16[2,256,256]{1,2,0:T(8,128)(2,1)S(1)}, bf16[2,256,256]{1,2,0:T(8,128)(2,1)S(1)}, u32[]{:S(2)}, u32[]{:S(2)}) %collective-permute-start.2) | collective-permute-done | bytes 262176 | tf_op jit(solution)/shard_map/ppermute | solution.py:16
  80.2 1.1 maximum_maximum_fusion
  81.2 0.9 fusion.29
  82.1 7.6 %fusion = (f32[2,8,256]{2,1,0:T(8,128)S(1)}, f32[2,1024,256,8]{2,1,3,0:T(8,128)}) fusion(pred[256,1024]{0,1:T(8,128)(4,1)S(1)} %and_and_fusion, bf16[1024,2,128,1]{0,2,3,1:T(8,128)(2,1)S(1)} %bitcast.70, bf16[256,2,8,64]{3,0,2,1:T(8,128)(2,1)S(1)} %bitcast.69, bf16[256,2,8,64]{3,0,2,1:T(8,128)(2,1)S(1)} %bitcast.68), kind=kOutput, calls=%fused_computation.2 | convolution fusion | flops 1088417792 | bytes 18628608 | tf_op jit(solution)/shard_map/while/body/eval_jaxpr/qkgd,skd->kgqs/dot_general | solution.py:66
  89.8 9.2 %fusion.3 = f32[2,8,256]{2,1,0:T(8,128)S(1)} fusion(f32[2,1024,256,8]{2,1,3,0:T(8,128)} %get-tuple-element.59, f32[2,8,256]{2,1,0:T(8,128)S(1)} %get-tuple-element.55, pred[256,1024]{0,1:T(8,128)(4,1)S(1)} %and_and_fusion), kind=kLoop, calls=%fused_computation.5 | loop fusion | flops 16773120 | bytes 17072128 | tf_op jit(solution)/shard_map/while/body/eval_jaxpr/reduce_sum | solution.py:76
  99.0 9.4 %fusion.12 = bf16[256,2,8,128]{0,3,2,1:T(8,128)(2,1)S(1)} fusion(bf16[1024,2,128,1]{0,2,3,1:T(8,128)(2,1)S(1)} %bitcast.77, f32[2,1024,256,8]{2,1,3,0:T(8,128)} %get-tuple-element.59, f32[2,8,256]{2,1,0:T(8,128)S(1)} %get-tuple-element.55, pred[256,1024]{0,1:T(8,128)(4,1)S(1)} %and_and_fusion, f32[256,2,8]{0,2,1:T(8,128)S(1)} %fusion.19, ...), kind=kOutput, calls=%fused_computation.18 | convolution fusion | flops 1092616192 | bytes 18661632 | tf_op jit(solution)/shard_map/while/body/eval_jaxpr/kgqs,skd->qkgd/dot_general | solution.py:77
  108.4 1.4 %copy.42 = bf16[1,256,2048]{2,1,0:T(8,128)(2,1)} copy(bf16[1,256,2048]{1,2,0:T(8,128)(2,1)S(1)} %bitcast.75) | data formatting | bytes 2097152
  109.8 1.2 %reduce_sum.26 = bf16[2,512,256]{2,1,0:T(8,128)(2,1)} reduce(bf16[4,2,512,256]{3,2,1,0:T(8,128)(2,1)S(1)} %all-to-all-done, bf16[]{:T(256)} %constant.50.clone.1), dimensions={0}, to_apply=%region_2.0 | reduce | flops 786432 | bytes 2621442 | tf_op jit(solution)/shard_map/reduce_sum | solution.py:131
  (26 shorter events, 1.2 us)
Async XLA Ops:
  3.0 19.8 %collective-permute-start = (bf16[2,256,256]{1,2,0:T(8,128)(2,1)}, bf16[2,256,256]{1,2,0:T(8,128)(2,1)}, u32[]{:S(2)}, u32[]{:S(2)}) collective-permute-start(bf16[2,256,256]{1,2,0:T(8,128)(2,1)} %pad_maximum_fusion.1), channel_id=1, source_target_pairs={{0,4},{4,8},{8,12},{1,5},{5,9},{9,13},{2,6},{6,10},{10,14},{3,7},{... | collective-permute-start | bytes 786440 | tf_op jit(solution)/shard_map/ppermute | solution.py:16
  15.2 6.3 %copy-start = (bf16[1,256,2048]{2,1,0:T(8,128)(2,1)S(1)}, bf16[1,256,2048]{2,1,0:T(8,128)(2,1)}, u32[]{:S(2)}) copy-start(bf16[1,256,2048]{2,1,0:T(8,128)(2,1)} %param.3) | copy-start | bytes 3145732
  15.2 94.6 %all-to-all-start = ((bf16[4,2,512,256]{3,2,1,0:T(8,128)(2,1)}), bf16[4,2,512,256]{3,2,1,0:T(8,128)(2,1)S(1)}, u32[]{:S(2)}, u32[]{:S(2)}) async-start(bf16[4,2,512,256]{3,2,1,0:T(8,128)(2,1)} %pad_maximum_fusion), calls=%async_computation | async-start | bytes 4194304 | tf_op jit(solution)/shard_map/all_to_all | solution.py:126
  22.1 4.1 %copy-start.1 = (f32[256,64]{1,0:T(8,128)S(1)}, f32[256,64]{1,0:T(8,128)}, u32[]{:S(2)}) copy-start(f32[256,64]{1,0:T(8,128)} %copy.38) | copy-start | bytes 196612
  22.1 4.1 %copy-start.2 = (f32[256,64]{1,0:T(8,128)S(1)}, f32[256,64]{1,0:T(8,128)}, u32[]{:S(2)}) copy-start(f32[256,64]{1,0:T(8,128)} %copy.36) | copy-start | bytes 196612
  22.8 48.6 %collective-permute-start.1 = (bf16[2,256,256]{1,2,0:T(8,128)(2,1)}, bf16[2,256,256]{1,2,0:T(8,128)(2,1)S(1)}, u32[]{:S(2)}, u32[]{:S(2)}) collective-permute-start(bf16[2,256,256]{1,2,0:T(8,128)(2,1)} %collective-permute-done), channel_id=1, source_target_pairs={{0,4},{4,8},{8,12},{1,5},{5,9},{9,13},{2,6},{6,10},{10,14},{3,7},{... | collective-permute-start | bytes 786440 | tf_op jit(solution)/shard_map/ppermute | solution.py:16
  71.4 8.7 %collective-permute-start.2 = (bf16[2,256,256]{1,2,0:T(8,128)(2,1)S(1)}, bf16[2,256,256]{1,2,0:T(8,128)(2,1)S(1)}, u32[]{:S(2)}, u32[]{:S(2)}) collective-permute-start(bf16[2,256,256]{1,2,0:T(8,128)(2,1)S(1)} %collective-permute-done.1), channel_id=1, source_target_pairs={{0,4},{4,8},{8,12},{1,5},{5,9},{9,13},{2,6},{6,10},{10,14},{3,7},{... | collective-permute-start | bytes 786440 | tf_op jit(solution)/shard_map/ppermute | solution.py:16
  89.8 9.2 %copy-start.3 = (bf16[1,1024,256]{1,2,0:T(8,128)(2,1)S(1)}, bf16[1,1024,256]{1,2,0:T(8,128)(2,1)}, u32[]{:S(2)}) copy-start(bf16[1,1024,256]{1,2,0:T(8,128)(2,1)} %get-tuple-element.49) | copy-start | bytes 1572868
